TPU v7x, 256 devices: a whole 4x4x8 slice. The times are simulated.
256 devices in a mesh: row: 16 (over z_hi, y, core), col: 16 (over x, z_lo).
Axes of the slice: x: 4, y: 4, z: 8 (z_hi: 2, z_lo: 4; z = z_hi * 4 + z_lo), core: 2. Of those that a mesh axis runs over, the one named last changes fastest.
Arguments:
- coefficients: float32 [8192, 8192], P('row', 'col'), may hold values from -6 to 6
- alpha_pattern: int32 [16, 10], P('row'), may hold values from 0 to 15, all different within a row
- alpha_count: int32 [16], P('row'), may hold values from 1 to 10
- alpha_blocks: bfloat16 [16, 10, 512, 512], P('row'), may hold values from -0.078125 to 0.078125
- beta_pattern: int32 [16, 10], P('col'), may hold values from 0 to 15, all different within a row
- beta_count: int32 [16], P('col'), may hold values from 1 to 10
- beta_blocks: bfloat16 [16, 10, 512, 512], P('col'), may hold values from -0.078125 to 0.078125
Outputs:
- sigma: float32 [8192, 8192], P('row', 'col')
Inputs may be any that keep to these rules, and one draw needn't show every extreme that they name: `alpha_pattern`: each row lists 10 different blocks, and every block stands in some row. `beta_pattern`: each row lists 10 different blocks, and every block stands in some row.
All inputs are finite; a program needn't handle non-finite values.
Results may differ from a plain program's by a relative error of at most 0.0029.
Values may be sent and summed in bfloat16 or wider, within the bound.
No kernel may reach another device: no remote copies, remote signals or barrier semaphores. Data moves between devices by JAX's collectives and lax.ppermute only.
A program may use at most 128 MiB of HBM per device.

v0:
```python
import jax
import jax.numpy as jnp
from jax import lax
from jax.sharding import PartitionSpec as P


def slot_mask(count, slots):
    return lax.broadcasted_iota(jnp.int32, (count.shape[0], slots), 1) < count[:, None]


def body(
    coefficients, alpha_pattern, alpha_count, alpha_blocks, beta_pattern, beta_count, beta_blocks
):
    coeff_bf = coefficients.astype(jnp.bfloat16)
    tile_rows, tile_cols = coeff_bf.shape
    slots = alpha_blocks.shape[1]
    block = alpha_blocks.shape[2]
    strings = tile_rows * lax.axis_size("row")
    blocks_all = strings // block
    alpha_mask = slot_mask(alpha_count, slots).astype(jnp.bfloat16)
    beta_mask = slot_mask(beta_count, slots).astype(jnp.bfloat16)
    column_slab = lax.all_gather(coeff_bf, "row", axis=0, tiled=True)
    row_slab = lax.all_gather(coeff_bf, "col", axis=1, tiled=True)
    slab_blocks = column_slab.reshape(blocks_all, block, tile_cols)
    slab_cols = row_slab.reshape(tile_rows, blocks_all, block)
    weighted = alpha_blocks * alpha_mask[:, :, None, None]
    picked = slab_blocks[alpha_pattern]
    alpha_term = jnp.einsum("itab,itbc->iac", weighted, picked, preferred_element_type=jnp.float32)
    beta_weighted = beta_blocks * beta_mask[:, :, None, None]
    beta_picked = slab_cols[:, beta_pattern, :]
    beta_term = jnp.einsum(
        "abtk,btck->bac", beta_picked, beta_weighted, preferred_element_type=jnp.float32
    )
    alpha_term = alpha_term.reshape(tile_rows, tile_cols)
    beta_term = jnp.transpose(beta_term, (1, 0, 2)).reshape(tile_rows, tile_cols)
    return alpha_term + beta_term


def solution(mesh):
    placed = (
        P("row", "col"),
        P("row", None),
        P("row"),
        P("row", None, None, None),
        P("col", None),
        P("col"),
        P("col", None, None, None),
    )
    return jax.shard_map(
        body, mesh=mesh, in_specs=placed, out_specs=P("row", "col"), check_vma=False
    )
```

profile of v0, /device:TPU:1, one launch (start us, length us, event | category | flops | bytes accessed | tf_op | source)
XLA Modules:
  0.0 356.1 jit_solution(14214862564943844612)
XLA Ops:
  6.5 0.0 all-gather.5.cloned.1.call-start
  6.5 2.2 copy.10
  8.8 0.0 all-gather.5.cloned.1.call-update
  8.8 0.0 all-gather.3.cloned.1.call-start
  8.8 0.7 all-gather.3.cloned.1.call-update
  10.9 0.7 fusion.22
  11.5 0.7 fusion.23
  12.2 185.9 %all-gather.5.cloned.1.call-done = bf16[512,8192]{0,1:T(8,128)(2,1)} async-done(((bf16[512,512]{0,1:T(8,128)(2,1)}), bf16[512,8192]{0,1:T(8,128)(2,1)}) %all-gather.5.cloned.1.call-update) | async-done | bytes 8388624 | tf_op jit(solution)/shard_map/all_gather | solution.py:23
  198.1 12.3 %copy.12 = bf16[512,16,512]{2,0,1:T(8,128)(2,1)} copy(bf16[512,16,512]{0,2,1:T(8,128)(2,1)} %bitcast.37) | data formatting | bytes 16777216 | tf_op jit(solution)/shard_map/reshape | solution.py:25
  210.4 101.7 %all-gather.3.cloned.1.call-done = bf16[8192,512]{0,1:T(8,128)(2,1)} async-done(((bf16[512,512]{0,1:T(8,128)(2,1)}), bf16[8192,512]{0,1:T(8,128)(2,1)}) %all-gather.3.cloned.1.call-update) | async-done | bytes 8388624 | tf_op jit(solution)/shard_map/all_gather | solution.py:22
  312.1 11.9 %copy.11 = bf16[8192,512]{1,0:T(8,128)(2,1)} copy(bf16[8192,512]{0,1:T(8,128)(2,1)} %all-gather.3.cloned.1.call-done) | data formatting | bytes 16777216 | tf_op jit(solution)/shard_map/all_gather | solution.py:22
  324.0 7.2 %gather_fusion = bf16[10,512,512]{2,1,0:T(8,128)(2,1)} fusion(bf16[16,512,512]{2,1,0:T(8,128)(2,1)} %bitcast.36, s32[1024]{0:T(1024)S(1)} %pad_clamp_fusion.1), kind=kCustom, calls=%fused_computation | custom fusion | bytes 10485800 | tf_op jit(solution)/shard_map/gather | solution.py:27
  331.2 0.0 slice-start
  331.2 7.3 %gather_fusion.1 = bf16[10,512,512]{2,1,0:T(8,128)(2,1)} fusion(bf16[512,16,512]{2,0,1:T(8,128)(2,1)} %copy.12, s32[1024]{0:T(1024)S(1)} %pad_clamp_fusion), kind=kCustom, calls=%fused_computation.1 | custom fusion | bytes 10485800 | tf_op jit(solution)/shard_map/gather | solution.py:30
  338.5 0.0 copy-start
  338.5 0.0 slice-start.1
  338.6 6.6 %fusion.9 = f32[512,512]{1,0:T(8,128)S(1)} fusion(bf16[10,512,512]{2,1,0:T(8,128)(2,1)} %gather_fusion, bf16[1,10,512,512]{3,2,1,0:T(8,128)(2,1)} %param.10, bf16[10]{0:T(256)(128)(2,1)S(1)} %compare_convert_fusion.1), kind=kOutput, calls=%fused_computation.11 | convolution fusion | flops 2686976000 | bytes 11534356 | tf_op jit(solution)/shard_map/itab,itbc->iac/dot_general | solution.py:28
  345.1 0.0 slice-done
  345.1 0.0 copy-done
  345.1 0.2 slice-done.1
  345.3 4.0 %fusion.17 = f32[512,512]{1,0:T(8,128)} fusion(f32[512,512]{1,0:T(8,128)S(1)} %fusion.9, bf16[1,10,512,512]{3,2,1,0:T(8,128)(2,1)S(1)} %bitcast.39, bf16[10]{0:T(256)(128)(2,1)S(1)} %compare_convert_fusion, bf16[10,512,512]{2,1,0:T(8,128)(2,1)S(1)} %copy-done), kind=kOutput, calls=%fused_computation.13 | convolution fusion | flops 2687238144 | bytes 12582932 | tf_op jit(solution)/shard_map/abtk,btck->bac/dot_general | solution.py:31
  (5 shorter events, 0.0 us)
Async XLA Ops:
  6.5 191.5 %all-gather.5.cloned.1.call-start = ((), (), s32[]{:S(2)}) async-start(), calls=%async_computation.1 | async-start | bytes 8912896 | tf_op jit(solution)/shard_map/all_gather | solution.py:23
  8.8 303.3 %all-gather.3.cloned.1.call-start = ((), (), s32[]{:S(2)}) async-start(), calls=%async_computation | async-start | bytes 8912896 | tf_op jit(solution)/shard_map/all_gather | solution.py:22
  331.2 13.9 %slice-start = ((s8[5242880]{0:T(1024)(128)(4,1)}), s8[1048576]{0:T(1024)(128)(4,1)S(1)}, s32[]{:S(2)}) async-start(s8[5242880]{0:T(1024)(128)(4,1)} %bitcast.38), calls=%async_computation.2 | async-start | bytes 2097152
  338.5 6.6 %copy-start = (bf16[10,512,512]{2,1,0:T(8,128)(2,1)S(1)}, bf16[10,512,512]{2,1,0:T(8,128)(2,1)}, u32[]{:S(2)}) copy-start(bf16[10,512,512]{2,1,0:T(8,128)(2,1)} %gather_fusion.1) | copy-start | bytes 15728644
  338.5 6.8 %slice-start.1 = ((s8[5242880]{0:T(1024)(128)(4,1)}), s8[4194304]{0:T(1024)(128)(4,1)S(1)}, s32[]{:S(2)}) async-start(s8[5242880]{0:T(1024)(128)(4,1)} %bitcast.38), calls=%async_computation.3 | async-start | bytes 8388608
Sparse Core Ops, SparseCore 0:
  9.1 188.8 all-gather.4
  200.6 111.4 all-gather.2
where the time goes:
time: 357 us; the launch traced here: 356 us
  waiting for transfers between devices  288 us (81%)
  local copies, waits for them, and re-layouts  41.2 us (12%)
  between operations  14.7 us (4%)
  matrix products  10.5 us (3%)
    all_gather x1, waiting for transfers between devices, body(): row_slab = lax.all_gather(coeff_bf, 'col', axis=1, tiled=True)  186 us
    all_gather x1, waiting for transfers between devices, body(): column_slab = lax.all_gather(coeff_bf, 'row', axis=0, tiled=True)  102 us
    reshape x1, local copies, waits for them, and re-layouts, body(): slab_cols = row_slab.reshape(tile_rows, blocks_all, block)  12.3 us
    all_gather x1, local copies, waits for them, and re-layouts, body(): column_slab = lax.all_gather(coeff_bf, 'row', axis=0, tiled=True)  11.9 us
    gather x1, local copies, waits for them, and re-layouts, body(): beta_picked = slab_cols[:, beta_pattern, :]  7.34 us
    gather x1, local copies, waits for them, and re-layouts, body(): picked = slab_blocks[alpha_pattern]  7.22 us
  transfers between devices with their start and end apart: 2, of which 2 were waited for; matrix products, arithmetic and copies ran while one was open for 4% of the time, Pallas kernels for 0%

commit v1 on v0

--- a/solution.py
+++ b/solution.py
@@ -20,7 +20,9 @@
     alpha_mask = slot_mask(alpha_count, slots).astype(jnp.bfloat16)
     beta_mask = slot_mask(beta_count, slots).astype(jnp.bfloat16)
     column_slab = lax.all_gather(coeff_bf, "row", axis=0, tiled=True)
-    row_slab = lax.all_gather(coeff_bf, "col", axis=1, tiled=True)
+    row_slab = jnp.concatenate(
+        lax.all_to_all(jnp.stack([coeff_bf] * lax.axis_size("col")), "col", 0, 0), axis=1
+    )
     slab_blocks = column_slab.reshape(blocks_all, block, tile_cols)
     slab_cols = row_slab.reshape(tile_rows, blocks_all, block)
     weighted = alpha_blocks * alpha_mask[:, :, None, None]

time: 357 us -> 289 us (0.81)
  waiting for transfers between devices: 288 us -> 232 us
  local copies, waits for them, and re-layouts: 41.2 us -> 20 us
  starting transfers between devices: 0.04 us -> 9.19 us
    all_gather x1 -> x0, waiting for transfers between devices: 186 us -> none  [body(): row_slab = lax.all_gather(coeff_bf, 'col', axis=1, tiled=True)]
    all_to_all x0 -> x1, waiting for transfers between devices: none -> 123 us  [body(): lax.all_to_all(jnp.stack([coeff_bf] * lax.axis_size('col')), 'col', 0, 0)]
    reshape x1 -> x0, local copies, waits for them, and re-layouts: 12.3 us -> none  [body(): slab_cols = row_slab.reshape(tile_rows, blocks_all, block)]
    all_gather x1 -> x0, local copies, waits for them, and re-layouts: 11.9 us -> none  [body(): column_slab = lax.all_gather(coeff_bf, 'row', axis=0, tiled=True)]
    all_to_all x0 -> x1, starting transfers between devices: none -> 9.19 us  [body(): lax.all_to_all(jnp.stack([coeff_bf] * lax.axis_size('col')), 'col', 0, 0)]
    all_gather x1, waiting for transfers between devices: 102 us -> 109 us  [body(): column_slab = lax.all_gather(coeff_bf, 'row', axis=0, tiled=True)]
    another operation x0 -> x1, local copies, waits for them, and re-layouts: none -> 5.07 us  [body(): jnp.stack([coeff_bf] * lax.axis_size('col'))]
where the time goes in v1:
time: 289 us
  waiting for transfers between devices  232 us (80%)
  local copies, waits for them, and re-layouts  20 us (7%)
  between operations  14.8 us (5%)
  matrix products  10.5 us (4%)
  starting transfers between devices  9.19 us (3%)
    all_to_all x1, waiting for transfers between devices, body(): lax.all_to_all(jnp.stack([coeff_bf] * lax.axis_size('col')), 'col', 0, 0)  123 us
    all_gather x1, waiting for transfers between devices, body(): column_slab = lax.all_gather(coeff_bf, 'row', axis=0, tiled=True)  109 us
    all_to_all x1, starting transfers between devices, body(): lax.all_to_all(jnp.stack([coeff_bf] * lax.axis_size('col')), 'col', 0, 0)  9.19 us
    gather x1, local copies, waits for them, and re-layouts, body(): beta_picked = slab_cols[:, beta_pattern, :]  7.41 us
    gather x1, local copies, waits for them, and re-layouts, body(): picked = slab_blocks[alpha_pattern]  7.32 us
    dot_general x1, matrix products, body(): jnp.einsum('itab,itbc->iac', weighted, picked, preferred_element_type=jnp...  6.56 us
  transfers between devices with their start and end apart: 2, of which 2 were waited for; matrix products, arithmetic and copies ran while one was open for 4% of the time, Pallas kernels for 0%

profile of v1, /device:TPU:1, one launch (start us, length us, event | category | flops | bytes accessed | tf_op | source)
XLA Modules:
  0.0 288.8 jit_solution(16016620359970388262)
XLA Ops:
  6.5 0.0 all-gather.2.cloned.1.call-start
  6.5 2.1 convert_element_type.22
  8.6 0.0 all-gather.2.cloned.1.call-update
  8.6 5.1 %stack.2 = bf16[16,512,512]{2,1,0:T(8,128)(2,1)} broadcast(bf16[512,512]{1,0:T(8,128)(2,1)} %convert_element_type.22), dimensions={1,2} | broadcast | bytes 8912896 | tf_op jit(solution)/shard_map/stack | solution.py:24
  13.7 0.0 copy-start.1
  13.7 0.0 copy-start.2
  13.7 9.2 %all-to-all-start = ((bf16[16,512,512]{2,1,0:T(8,128)(2,1)}), bf16[16,512,512]{2,1,0:T(8,128)(2,1)}, u32[]{:S(2)}, u32[]{:S(2)}) async-start(bf16[16,512,512]{2,1,0:T(8,128)(2,1)} %stack.2), calls=%async_computation | async-start | bytes 16777216 | tf_op jit(solution)/shard_map/all_to_all | solution.py:24
  24.2 0.0 copy-done.1
  24.3 0.0 copy-done.2
  24.3 109.5 %all-gather.2.cloned.1.call-done = bf16[8192,512]{1,0:T(8,128)(2,1)} async-done(((bf16[512,512]{1,0:T(8,128)(2,1)}), bf16[8192,512]{1,0:T(8,128)(2,1)}) %all-gather.2.cloned.1.call-update) | async-done | bytes 8388624 | tf_op jit(solution)/shard_map/all_gather | solution.py:22
  133.8 7.3 %gather_fusion = bf16[10,512,512]{2,1,0:T(8,128)(2,1)} fusion(bf16[16,512,512]{2,1,0:T(8,128)(2,1)} %bitcast.36, s32[1024]{0:T(1024)S(1)} %pad_clamp_fusion.1), kind=kCustom, calls=%fused_computation | custom fusion | bytes 10485800 | tf_op jit(solution)/shard_map/gather | solution.py:29
  141.1 122.7 %all-to-all-done = bf16[16,512,512]{2,1,0:T(8,128)(2,1)} async-done(((bf16[16,512,512]{2,1,0:T(8,128)(2,1)}), bf16[16,512,512]{2,1,0:T(8,128)(2,1)}, u32[]{:S(2)}, u32[]{:S(2)}) %all-to-all-start) | async-done | bytes 8388640 | tf_op jit(solution)/shard_map/all_to_all | solution.py:24
  263.8 0.0 slice-start
  263.8 7.4 %gather_fusion.1 = bf16[10,512,512]{2,1,0:T(8,128)(2,1)} fusion(bf16[512,16,512]{2,0,1:T(8,128)(2,1)} %bitcast.5, s32[1024]{0:T(1024)S(1)} %pad_clamp_fusion), kind=kCustom, calls=%fused_computation.1 | custom fusion | bytes 10485800 | tf_op jit(solution)/shard_map/gather | solution.py:32
  271.2 0.0 copy-start
  271.2 0.0 slice-start.1
  271.2 6.6 %fusion.9 = f32[512,512]{1,0:T(8,128)S(1)} fusion(bf16[10,512,512]{2,1,0:T(8,128)(2,1)} %gather_fusion, bf16[1,10,512,512]{3,2,1,0:T(8,128)(2,1)} %param.10, bf16[10]{0:T(256)(128)(2,1)S(1)} %compare_convert_fusion.1), kind=kOutput, calls=%fused_computation.11 | convolution fusion | flops 2686976000 | bytes 11534356 | tf_op jit(solution)/shard_map/itab,itbc->iac/dot_general | solution.py:30
  277.8 0.0 slice-done
  277.8 0.0 copy-done
  277.8 0.2 slice-done.1
  278.0 4.0 %fusion.17 = f32[512,512]{1,0:T(8,128)} fusion(f32[512,512]{1,0:T(8,128)S(1)} %fusion.9, bf16[1,10,512,512]{3,2,1,0:T(8,128)(2,1)S(1)} %bitcast.38, bf16[10]{0:T(256)(128)(2,1)S(1)} %compare_convert_fusion, bf16[10,512,512]{2,1,0:T(8,128)(2,1)S(1)} %copy-done), kind=kOutput, calls=%fused_computation.13 | convolution fusion | flops 2687238144 | bytes 12582932 | tf_op jit(solution)/shard_map/abtk,btck->bac/dot_general | solution.py:33
  (7 shorter events, 0.0 us)
Async XLA Ops:
  6.5 127.3 %all-gather.2.cloned.1.call-start = ((), (), s32[]{:S(2)}) async-start(), calls=%async_computation.1 | async-start | bytes 8912896 | tf_op jit(solution)/shard_map/all_gather | solution.py:22
  13.7 10.5 %copy-start.1 = (s32[1,10]{1,0:T(1,128)S(1)}, s32[1,10]{1,0:T(1,128)}, u32[]{:S(2)}) copy-start(s32[1,10]{1,0:T(1,128)} %param.8) | copy-start | bytes 124
  13.7 10.6 %copy-start.2 = (s32[1,10]{1,0:T(1,128)S(1)}, s32[1,10]{1,0:T(1,128)}, u32[]{:S(2)}) copy-start(s32[1,10]{1,0:T(1,128)} %param.11) | copy-start | bytes 124
  13.7 250.1 %all-to-all-start = ((bf16[16,512,512]{2,1,0:T(8,128)(2,1)}), bf16[16,512,512]{2,1,0:T(8,128)(2,1)}, u32[]{:S(2)}, u32[]{:S(2)}) async-start(bf16[16,512,512]{2,1,0:T(8,128)(2,1)} %stack.2), calls=%async_computation | async-start | bytes 16777216 | tf_op jit(solution)/shard_map/all_to_all | solution.py:24
  263.8 14.0 %slice-start = ((s8[5242880]{0:T(1024)(128)(4,1)}), s8[1048576]{0:T(1024)(128)(4,1)S(1)}, s32[]{:S(2)}) async-start(s8[5242880]{0:T(1024)(128)(4,1)} %bitcast.37), calls=%async_computation.2 | async-start | bytes 2097152
  271.2 6.6 %copy-start = (bf16[10,512,512]{2,1,0:T(8,128)(2,1)S(1)}, bf16[10,512,512]{2,1,0:T(8,128)(2,1)}, u32[]{:S(2)}) copy-start(bf16[10,512,512]{2,1,0:T(8,128)(2,1)} %gather_fusion.1) | copy-start | bytes 15728644
  271.2 6.8 %slice-start.1 = ((s8[5242880]{0:T(1024)(128)(4,1)}), s8[4194304]{0:T(1024)(128)(4,1)S(1)}, s32[]{:S(2)}) async-start(s8[5242880]{0:T(1024)(128)(4,1)} %bitcast.37), calls=%async_computation.3 | async-start | bytes 8388608
Sparse Core Ops, SparseCore 0:
  10.1 123.6 all-gather.1
